TPU v7x, 256 devices: a whole 4x4x8 slice. The times are simulated.
256 devices in a mesh: group: 8 (over x, core), inner: 32 (over z, y).
Axes of the slice: x: 4, y: 4, z: 8, core: 2. Of those that a mesh axis runs over, the one named last changes fastest.
Arguments:
- flow_field: float32 [1536, 1536, 128], P('inner', 'group'), may hold values from -6 to 6
- sketch_rows: float32 [1536, 128], P('inner'), may hold values from -6 to 6
- sketch_cols: float32 [1536, 128], P('group'), may hold values from -6 to 6
- sketch_depth: float32 [128, 128], replicated, may hold values from -6 to 6
- bit_widths: int32 [2], replicated, may hold values from 6 to 8
- bin_edges: int32 [9], replicated, may hold values from -6 to 6, as said below
Outputs:
- basis_one: float32 [1536, 128], P('inner')
- basis_two: float32 [1536, 128], P('group')
- core: float32 [128, 128, 128], P('inner', 'group')
- residual: float32 [2, 128, 128, 128], P(None, 'inner', 'group')
- energy: float32 [2, 1536, 128], P(None, 'inner')
- histogram: float32 [2, 1536, 8], P(None, 'inner')
Inputs may be any that keep to these rules, and one draw needn't show every extreme that they name: `bin_edges`: strictly increasing; the first is -6 and the last 6.
All inputs are finite; a program needn't handle non-finite values.
Results may differ from a plain program's by a relative error of at most 0.0008.
Values sent between devices are 32-bit elements; how exact they have to be, the bound alone decides.
No kernel may reach another device: no remote copies, remote signals or barrier semaphores. Data moves between devices by JAX's collectives and lax.ppermute only.
A program may use at most 128 MiB of HBM per device.

v0:
```python
import math
import jax
import jax.numpy as jnp
from jax import lax
from jax.sharding import PartitionSpec as P

N1 = 1536
N2 = 1536
N3 = 128
R = 128
NEDGE = 9
NBINS = 8
precise = lax.Precision.HIGHEST
two_pi = 2.0 * 3.141592653589793
error_boost = 16.0


def gram_of(sketch):
    return jnp.dot(sketch.T, sketch, precision=precise)


def orthonormal_rows(sketch, gram_matrix):
    lower_factor = jnp.linalg.cholesky(gram_matrix)
    return jax.scipy.linalg.solve_triangular(lower_factor, sketch.T, lower=True).T


def soft_residual(core_values, step_size):
    return -jnp.sin(two_pi * core_values[None] / step_size[:, None, None, None]) / two_pi


def local(flow_field, sketch_rows, sketch_cols, sketch_depth, bit_widths, bin_edges):
    reduced = jnp.einsum("ijk,kr->ijr", flow_field, sketch_depth, precision=precise)
    mode_one = jnp.einsum("ijr,jr->ir", reduced, sketch_cols, precision=precise)
    mode_two = jnp.einsum("ijr,ir->jr", reduced, sketch_rows, precision=precise)
    mode_one = lax.psum(mode_one, "group")
    basis_one = orthonormal_rows(mode_one, lax.psum(gram_of(mode_one), "inner"))
    mode_two = lax.psum(mode_two, "inner")
    basis_two = orthonormal_rows(mode_two, lax.psum(gram_of(mode_two), "group"))
    along_two = jnp.einsum("ijk,js->isk", flow_field, basis_two, precision=precise)
    levels = jnp.exp2(bit_widths.astype(jnp.float32) - 1.0) - 1.0
    summed_two = lax.psum_scatter(along_two, "group", scatter_dimension=1, tiled=True)
    partial_rows = jnp.einsum("ir,isk->rsk", basis_one, summed_two, precision=precise)
    core_shard = lax.psum_scatter(partial_rows, "inner", scatter_dimension=0, tiled=True)
    peak = lax.pmax(jnp.max(jnp.abs(core_shard)), ("group", "inner"))
    residual_shard = soft_residual(core_shard, peak / levels)
    spread = lax.all_gather(residual_shard, "group", axis=2, tiled=True)
    mixed_core = jnp.einsum(
        "ir,brsk->bisk",
        basis_one,
        lax.all_gather(spread, "inner", axis=1, tiled=True),
        precision=precise,
    )
    error_scale = error_boost * math.sqrt(N1 * N2) / R
    field_error = error_scale * jnp.einsum(
        "bisk,js->bijk", mixed_core, basis_two, precision=precise
    )
    energy_part = jnp.sum(field_error * field_error, axis=2) / N2
    edge_values = bin_edges.astype(jnp.float32)
    ramp_part = jnp.stack(
        [
            jnp.sum(jnp.clip(field_error - edge_values[index_edge] + 0.5, 0.0, 1.0), axis=(2, 3))
            for index_edge in range(NEDGE)
        ],
        axis=-1,
    )
    energy, ramp_sums = lax.psum((energy_part, ramp_part), "group")
    histogram = (ramp_sums[..., :-1] - ramp_sums[..., 1:]) * (NBINS / (N2 * N3))
    return (basis_one, basis_two, core_shard, residual_shard, energy, histogram)


def solution(mesh):
    in_specs = (P("inner", "group", None), P("inner", None), P("group", None), P(), P(), P())
    out_specs = (
        P("inner", None),
        P("group", None),
        P("inner", "group", None),
        P(None, "inner", "group", None),
        P(None, "inner", None),
        P(None, "inner", None),
    )
    return jax.shard_map(local, mesh=mesh, in_specs=in_specs, out_specs=out_specs, check_vma=False)
```

profile of v0, /device:TPU:8, one launch (start us, length us, event | category | flops | bytes accessed | tf_op | source)
XLA Modules:
  0.0 863.6 jit_solution(15359649875850458368)
XLA Ops:
  7.2 0.8 copy-done
  8.0 7.1 multiply_reduce_fusion.2
  15.2 26.1 %psum.42 = f32[48,128]{0,1:T(8,128)S(1)} all-reduce(f32[48,128]{0,1:T(8,128)S(1)} %bitcast.98), channel_id=1, replica_groups=mesh['group'=8,'inner'=32] {'group'}, use_global_device_ids=true, to_apply=%region_0.0 | all-reduce | flops 6144 | bytes 49152 | tf_op jit(solution)/shard_map/psum | solution.py:35
  41.3 0.9 fusion.25
  42.2 2.8 multiply_reduce_fusion.1
  45.0 0.8 copy.39
  45.8 143.9 %all-reduce.7.cloned.1.call-done = (f32[128,128]{0,1:T(8,128)}, f32[192,128]{0,1:T(8,128)}) async-done(((f32[128,128]{0,1:T(8,128)}, f32[192,128]{0,1:T(8,128)}), (f32[128,128]{0,1:T(8,128)}, f32[192,128]{0,1:T(8,128)})) %all-reduce.7.cloned.1.call-update) | async-done | bytes 163856 | tf_op jit(solution)/shard_map/psum | solution.py:36
  189.7 1.9 fusion.26
  191.8 64.2 %all-reduce.5.cloned.1.call-done = f32[128,128]{0,1:T(8,128)} async-done(((f32[128,128]{0,1:T(8,128)}), f32[128,128]{0,1:T(8,128)}) %all-reduce.5.cloned.1.call-update) | async-done | bytes 65552 | tf_op jit(solution)/shard_map/psum | solution.py:38
  256.0 0.9 copy.22
  256.9 0.9 fusion.14
  257.8 11.7 %cholesky.55 = f32[128,128]{1,0:T(8,128)S(1)} custom-call(f32[128,128]{1,0:T(8,128)S(1)} %fusion.14), custom_call_target="Cholesky" | custom-call | tf_op jit(solution)/shard_map/jit(cholesky)/cholesky | solution.py:23
  270.2 0.7 fusion.11
  270.8 9.8 %custom-call.11 = f32[1,128,128]{1,2,0:T(8,128)S(1)} custom-call(f32[1,128,128]{2,1,0:T(8,128)S(1)} %fusion.11), custom_call_target="InvertDiagBlocksLowerTriangular" | custom-call | tf_op jit(solution)/shard_map/jit(_solve_triangular)/triangular_solve | solution.py:24
  280.6 1.3 fusion.12
  281.9 4.8 fusion.6
  286.8 3.5 copy.57
  290.7 11.7 %cholesky.44 = f32[128,128]{1,0:T(8,128)S(1)} custom-call(f32[128,128]{1,0:T(8,128)S(1)} %fusion.17), custom_call_target="Cholesky" | custom-call | tf_op jit(solution)/shard_map/jit(cholesky)/cholesky | solution.py:23
  303.1 0.7 fusion.10
  303.8 9.8 %custom-call.10 = f32[1,128,128]{1,2,0:T(8,128)S(1)} custom-call(f32[1,128,128]{2,1,0:T(8,128)S(1)} %fusion.10), custom_call_target="InvertDiagBlocksLowerTriangular" | custom-call | tf_op jit(solution)/shard_map/jit(_solve_triangular)/triangular_solve | solution.py:24
  313.9 14.2 %reduce-scatter.3.cloned.1.call-done = f32[48,16,128]{2,0,1:T(8,128)} async-done(((f32[48,128,128]{2,0,1:T(8,128)}), f32[48,16,128]{2,0,1:T(8,128)}) %reduce-scatter.3.cloned.1.call-update) | async-done | bytes 393232 | tf_op jit(solution)/shard_map/reduce_scatter | solution.py:41
  328.1 2.0 fusion.21
  330.1 1.6 copy.23
  331.8 215.3 %reduce-scatter.5.cloned.1.call-done = f32[4,16,128]{2,1,0:T(8,128)} async-done(((f32[128,16,128]{2,1,0:T(8,128)}), f32[4,16,128]{2,1,0:T(8,128)}) %reduce-scatter.5.cloned.1.call-update) | async-done | bytes 32784 | tf_op jit(solution)/shard_map/reduce_scatter | solution.py:43
  547.1 1.4 broadcast_multiply_fusion.2
  548.5 74.3 %pmax.7 = f32[]{:T(128)} all-reduce(f32[]{:T(128)} %get-tuple-element.34), channel_id=1, replica_groups=mesh['group'=8,'inner'=32] {'group','inner'}, use_global_device_ids=true, to_apply=%region_9.11 | all-reduce | flops 1 | bytes 8 | tf_op jit(solution)/shard_map/pmax | solution.py:44
  623.8 14.5 %all_gather.6 = f32[2,4,128,128]{3,2,1,0:T(8,128)} all-gather(f32[2,4,16,128]{3,2,1,0:T(8,128)S(1)} %fusion.9), channel_id=1, replica_groups=mesh['group'=8,'inner'=32] {'group'}, dimensions={2}, use_global_device_ids=true | all-gather | bytes 589824 | tf_op jit(solution)/shard_map/all_gather | solution.py:46
  638.3 0.7 fusion.24
  639.0 135.6 %all-gather.2.cloned.1.call-done = f32[2,128,128,128]{3,2,1,0:T(8,128)} async-done(((f32[2,4,128,128]{3,2,1,0:T(8,128)}), f32[2,128,128,128]{3,2,1,0:T(8,128)}) %all-gather.2.cloned.1.call-update) | async-done | bytes 16777232 | tf_op jit(solution)/shard_map/all_gather | solution.py:50
  774.6 22.9 %fusion = f32[2,128,128,48]{2,3,1,0:T(8,128)S(1)} fusion(f32[2,128,128,128]{3,2,1,0:T(8,128)} %all-gather.2.cloned.1.call-done, f32[128,48]{0,1:T(8,128)S(1)} %fusion.15), kind=kOutput, calls=%fused_computation | convolution fusion | flops 2415919104 | bytes 23093248 | tf_op jit(solution)/shard_map/ir,brsk->bisk/dot_general | solution.py:47
  797.5 32.9 %clamp_reduce_fusion = (f32[2,48]{1,0:T(2,128)S(1)}, f32[2,48]{1,0:T(2,128)S(1)}, f32[2,48]{1,0:T(2,128)S(1)}, f32[2,48]{1,0:T(2,128)S(1)}, f32[2,48]{1,0:T(2,12...) fusion(f32[]{:T(128)} %bitcast.39, f32[]{:T(128)} %bitcast.23, ...), kind=kOutput, calls=%fused_computation.2 | convolution fusion | flops 3715877888 | bytes 6442404 | tf_op jit(solution)/shard_map/bisk,js->bijk/dot_general | solution.py:54
  830.6 25.9 %all-reduce.1 = (f32[2,48,128]{2,1,0:T(8,128)}, f32[2,48,9]{1,0,2:T(2,128)S(1)}) all-reduce(f32[2,48,128]{2,1,0:T(8,128)S(1)} %broadcast_multiply_fusion.1, f32[2,48,9]{1,0,2:T(2,128)S(1)} %constant_dynamic-update-slice_fusion), channel_id=1, replica_groups=mesh['group'=8,'inner'=32] {'group'}, use_global_device_ids=true, to_apply=%region_11.13 | all-reduce | flops 13152 | bytes 105216 | tf_op jit(solution)/shard_map/psum | solution.py:66
  (48 shorter events, 4.2 us)
Async XLA Ops:
  7.2 0.8 copy-start
  7.2 35.0 %copy-start.5 = (f32[48,128]{1,0:T(8,128)S(1)}, f32[48,128]{1,0:T(8,128)}, u32[]{:S(2)}) copy-start(f32[48,128]{1,0:T(8,128)} %param.8) | copy-start | bytes 73732
  7.2 182.5 %all-reduce.7.cloned.1.call-start = ((), (), s32[]{:S(2)}) async-start(), calls=%async_computation.6 | async-start | bytes 393216 | tf_op jit(solution)/shard_map/psum | solution.py:36
  45.7 210.2 %all-reduce.5.cloned.1.call-start = ((), (), s32[]{:S(2)}) async-start(), calls=%async_computation.2 | async-start | bytes 131072 | tf_op jit(solution)/shard_map/psum | solution.py:38
  189.7 100.9 %copy-start.3 = (f32[128,128]{0,1:T(8,128)S(1)}, f32[128,128]{0,1:T(8,128)}, u32[]{:S(2)}) copy-start(f32[128,128]{0,1:T(8,128)} %get-tuple-element.29) | copy-start | bytes 196612
  191.6 136.5 %reduce-scatter.3.cloned.1.call-start = ((), (), s32[]{:S(2)}) async-start(), calls=%async_computation.3 | async-start | bytes 3538944 | tf_op jit(solution)/shard_map/reduce_scatter | solution.py:41
  281.9 515.6 %copy-start.1 = (f32[128,192]{0,1:T(8,128)}, f32[128,192]{0,1:T(8,128)S(1)}, u32[]{:S(2)}) copy-start(f32[128,192]{0,1:T(8,128)S(1)} %fusion.12) | copy-start | bytes 294916
  281.9 340.9 %copy-start.6 = (s32[2]{0:T(128)S(1)}, s32[2]{0:T(128)}, u32[]{:S(2)}) copy-start(s32[2]{0:T(128)} %param.11) | copy-start | bytes 28
  286.8 351.5 %copy-start.7 = (s32[9]{0:T(128)S(1)}, s32[9]{0:T(128)}, u32[]{:S(2)}) copy-start(s32[9]{0:T(128)} %param.12) | copy-start | bytes 112
  290.3 256.8 %reduce-scatter.5.cloned.1.call-start = ((), (), s32[]{:S(2)}) async-start(), calls=%async_computation.4 | async-start | bytes 1081344 | tf_op jit(solution)/shard_map/reduce_scatter | solution.py:43
  313.9 483.7 %copy-start.4 = (f32[128,48]{0,1:T(8,128)}, f32[128,48]{0,1:T(8,128)S(1)}, u32[]{:S(2)}) copy-start(f32[128,48]{0,1:T(8,128)S(1)} %fusion.15) | copy-start | bytes 73732
  331.7 442.9 %all-gather.2.cloned.1.call-start = ((), (), s32[]{:S(2)}) async-start(), calls=%async_computation.5 | async-start | bytes 17301504 | tf_op jit(solution)/shard_map/all_gather | solution.py:50
  623.8 173.7 %copy-start.2 = (f32[2,4,16,128]{3,2,1,0:T(8,128)}, f32[2,4,16,128]{3,2,1,0:T(8,128)S(1)}, u32[]{:S(2)}) copy-start(f32[2,4,16,128]{3,2,1,0:T(8,128)S(1)} %fusion.9) | copy-start | bytes 196612
Sparse Core Ops, SparseCore 0:
  45.9 143.7 all-reduce.6
  192.5 63.3 all-reduce.4
  290.4 37.5 reduce-scatter.2
  332.3 214.7 reduce-scatter.4
  638.4 136.1 all-gather.1
where the time goes:
time: 864 us
  waiting for transfers between devices  573 us (66%)
  blocking collectives  141 us (16%)
  matrix products  74.1 us (9%)
  other arithmetic  51.7 us (6%)
  between operations  14 us (2%)
  local copies, waits for them, and re-layouts  9.15 us (1%)
    reduce_scatter x1, waiting for transfers between devices, local(): lax.psum_scatter(partial_rows, 'inner', scatter_dimension=0, tiled=True)  215 us
    psum x1, waiting for transfers between devices, local(): basis_one = orthonormal_rows(mode_one, lax.psum(gram_of(mode_one), 'inner'))  144 us
    all_gather x1, waiting for transfers between devices, local(): lax.all_gather(spread, 'inner', axis=1, tiled=True)  136 us
    pmax x1, blocking collectives, local(): peak = lax.pmax(jnp.max(jnp.abs(core_shard)), ('group', 'inner'))  74.3 us
    psum x1, waiting for transfers between devices, local(): basis_two = orthonormal_rows(mode_two, lax.psum(gram_of(mode_two), 'group'))  64.2 us
    dot_general x1, matrix products, local(): jnp.einsum('bisk,js->bijk', mixed_core, basis_two, precision=precise)  32.9 us
    psum x1, blocking collectives, local(): mode_one = lax.psum(mode_one, 'group')  26.1 us
    psum x1, blocking collectives, local(): energy, ramp_sums = lax.psum((energy_part, ramp_part), 'group')  25.9 us
  transfers between devices with their start and end apart: 5, of which 5 were waited for; matrix products, arithmetic and copies ran while one was open for 3% of the time, Pallas kernels for 0%

commit v1 on v0

--- a/solution.py
+++ b/solution.py
@@ -44,10 +44,17 @@
     peak = lax.pmax(jnp.max(jnp.abs(core_shard)), ("group", "inner"))
     residual_shard = soft_residual(core_shard, peak / levels)
     spread = lax.all_gather(residual_shard, "group", axis=2, tiled=True)
+
+    def _bring_shifts_all(on_dim, x_part, lane_axis):
+        vec_out = jnp.stack(lax.axis_size(lane_axis) * [x_part])
+        t1 = lax.all_to_all(vec_out, lane_axis, 0, 0)
+        arr_now = jnp.concatenate(t1, axis=on_dim)
+        return arr_now
+
     mixed_core = jnp.einsum(
         "ir,brsk->bisk",
         basis_one,
-        lax.all_gather(spread, "inner", axis=1, tiled=True),
+        _bring_shifts_all(1, x_part=spread, lane_axis="inner"),
         precision=precise,
     )
     error_scale = error_boost * math.sqrt(N1 * N2) / R

time: 864 us -> 1150 us (1.33)
  the two profiles are of different devices: /device:TPU:8 before, /device:TPU:16 now
where the time goes in v1:
time: 1150 us
  waiting for transfers between devices  841 us (73%)
  blocking collectives  137 us (12%)
  matrix products  72.9 us (6%)
  other arithmetic  51.7 us (4%)
  local copies, waits for them, and re-layouts  20.3 us (2%)
  between operations  14.5 us (1%)
    all_to_all x1, waiting for transfers between devices, _bring_shifts_all(): t1 = lax.all_to_all(vec_out, lane_axis, 0, 0)  404 us
    reduce_scatter x1, waiting for transfers between devices, local(): lax.psum_scatter(partial_rows, 'inner', scatter_dimension=0, tiled=True)  215 us
    psum x1, waiting for transfers between devices, local(): basis_one = orthonormal_rows(mode_one, lax.psum(gram_of(mode_one), 'inner'))  144 us
    pmax x1, blocking collectives, local(): peak = lax.pmax(jnp.max(jnp.abs(core_shard)), ('group', 'inner'))  73.7 us
    psum x1, waiting for transfers between devices, local(): basis_two = orthonormal_rows(mode_two, lax.psum(gram_of(mode_two), 'group'))  64.1 us
    dot_general x1, matrix products, local(): jnp.einsum('bisk,js->bijk', mixed_core, basis_two, precision=precise)  32.9 us
    psum x1, blocking collectives, local(): mode_one = lax.psum(mode_one, 'group')  26.1 us
    another operation x6, other arithmetic, orthonormal_rows(): lower_factor = jnp.linalg.cholesky(gram_matrix)  24.8 us
  transfers between devices with their start and end apart: 5, of which 5 were waited for; matrix products, arithmetic and copies ran while one was open for 2% of the time, Pallas kernels for 0%

profile of v1, /device:TPU:16, one launch (start us, length us, event | category | flops | bytes accessed | tf_op | source)
XLA Modules:
  0.0 1147.9 jit_solution(17126635183540514190)
XLA Ops:
  7.2 0.8 copy-done
  8.0 7.1 multiply_reduce_fusion.2
  15.2 26.1 %psum.42 = f32[48,128]{0,1:T(8,128)S(1)} all-reduce(f32[48,128]{0,1:T(8,128)S(1)} %bitcast.96), channel_id=1, replica_groups=mesh['group'=8,'inner'=32] {'group'}, use_global_device_ids=true, to_apply=%region_0.0 | all-reduce | flops 6144 | bytes 49152 | tf_op jit(solution)/shard_map/psum | solution.py:35
  41.3 0.9 fusion.27
  42.2 2.8 multiply_reduce_fusion.1
  45.0 0.8 copy.50
  45.8 143.5 %all-reduce.7.cloned.1.call-done = (f32[128,128]{0,1:T(8,128)}, f32[192,128]{0,1:T(8,128)}) async-done(((f32[128,128]{0,1:T(8,128)}, f32[192,128]{0,1:T(8,128)}), (f32[128,128]{0,1:T(8,128)}, f32[192,128]{0,1:T(8,128)})) %all-reduce.7.cloned.1.call-update) | async-done | bytes 163856 | tf_op jit(solution)/shard_map/psum | solution.py:36
  189.3 1.9 fusion.28
  191.8 64.1 %all-reduce.5.cloned.1.call-done = f32[128,128]{0,1:T(8,128)} async-done(((f32[128,128]{0,1:T(8,128)}), f32[128,128]{0,1:T(8,128)}) %all-reduce.5.cloned.1.call-update) | async-done | bytes 65552 | tf_op jit(solution)/shard_map/psum | solution.py:38
  255.9 0.9 copy.29
  256.8 0.9 fusion.17
  257.7 11.7 %cholesky.55 = f32[128,128]{1,0:T(8,128)S(1)} custom-call(f32[128,128]{1,0:T(8,128)S(1)} %fusion.17), custom_call_target="Cholesky" | custom-call | tf_op jit(solution)/shard_map/jit(cholesky)/cholesky | solution.py:23
  270.8 9.8 custom-call.11
  280.6 1.3 fusion.15
  281.9 7.0 convolution_bitcast_fusion
  289.2 11.7 %cholesky.44 = f32[128,128]{1,0:T(8,128)S(1)} custom-call(f32[128,128]{1,0:T(8,128)S(1)} %fusion.20), custom_call_target="Cholesky" | custom-call | tf_op jit(solution)/shard_map/jit(cholesky)/cholesky | solution.py:23
  302.3 9.8 custom-call.10
  312.4 14.3 %reduce-scatter.3.cloned.1.call-done = f32[48,16,128]{2,1,0:T(8,128)} async-done(((f32[48,128,128]{2,1,0:T(8,128)}), f32[48,16,128]{2,1,0:T(8,128)}) %reduce-scatter.3.cloned.1.call-update) | async-done | bytes 393232 | tf_op jit(solution)/shard_map/reduce_scatter | solution.py:41
  326.7 2.0 fusion.7
  328.8 1.6 copy.31
  330.4 215.2 %reduce-scatter.5.cloned.1.call-done = f32[4,16,128]{2,1,0:T(8,128)} async-done(((f32[128,16,128]{2,1,0:T(8,128)}), f32[4,16,128]{2,1,0:T(8,128)}) %reduce-scatter.5.cloned.1.call-update) | async-done | bytes 32784 | tf_op jit(solution)/shard_map/reduce_scatter | solution.py:43
  545.6 1.4 broadcast_multiply_fusion.2
  547.0 73.7 %pmax.7 = f32[]{:T(128)} all-reduce(f32[]{:T(128)} %get-tuple-element.40), channel_id=1, replica_groups=mesh['group'=8,'inner'=32] {'group','inner'}, use_global_device_ids=true, to_apply=%region_9.11 | all-reduce | flops 1 | bytes 8 | tf_op jit(solution)/shard_map/pmax | solution.py:44
  621.6 13.1 %all_gather.3 = f32[2,4,128,128]{3,2,1,0:T(8,128)S(1)} all-gather(f32[2,4,16,128]{3,2,1,0:T(8,128)S(1)} %fusion.12), channel_id=1, replica_groups=mesh['group'=8,'inner'=32] {'group'}, dimensions={2}, use_global_device_ids=true | all-gather | bytes 589824 | tf_op jit(solution)/shard_map/all_gather | solution.py:46
  634.7 7.8 stack.22
  642.6 8.7 all-to-all-start
  651.3 0.7 fusion.26
  652.0 404.3 %all-to-all-done = f32[32,2,4,128,128]{4,3,2,1,0:T(8,128)} async-done(((f32[32,2,4,128,128]{4,3,2,1,0:T(8,128)}), f32[32,2,4,128,128]{4,3,2,1,0:T(8,128)}, u32[]{:S(2)}, u32[]{:S(2)}) %all-to-all-start) | async-done | bytes 16777248 | tf_op jit(solution)/shard_map/all_to_all | solution.py:50
  1056.3 6.8 copy.32
  1063.1 19.6 %fusion.4 = f32[2,48,128,128]{3,1,2,0:T(8,128)S(1)} fusion(f32[2,128,128,128]{3,2,1,0:T(8,128)S(1)} %bitcast.93, f32[128,48]{0,1:T(8,128)S(1)} %fusion.18), kind=kOutput, calls=%fused_computation.17 | convolution fusion | flops 2415919104 | bytes 23093248 | tf_op jit(solution)/shard_map/ir,brsk->bisk/dot_general | solution.py:54
  1082.7 32.9 %clamp_reduce_fusion = (f32[2,48]{1,0:T(2,128)S(1)}, f32[2,48]{1,0:T(2,128)S(1)}, f32[2,48]{1,0:T(2,128)S(1)}, f32[2,48]{1,0:T(2,128)S(1)}, f32[2,48]{1,0:T(2,12...) fusion(f32[]{:T(128)} %bitcast.41, f32[]{:T(128)} %bitcast.25, ...), kind=kOutput, calls=%fused_computation.2 | convolution fusion | flops 3715877888 | bytes 6442404 | tf_op jit(solution)/shard_map/bisk,js->bijk/dot_general | solution.py:61
  1115.7 24.6 %all-reduce.1 = (f32[2,48,128]{2,1,0:T(8,128)}, f32[2,48,9]{1,0,2:T(2,128)S(1)}) all-reduce(f32[2,48,128]{2,1,0:T(8,128)S(1)} %broadcast_multiply_fusion.1, f32[2,48,9]{1,0,2:T(2,128)S(1)} %constant_dynamic-update-slice_fusion), channel_id=1, replica_groups=mesh['group'=8,'inner'=32] {'group'}, use_global_device_ids=true, to_apply=%region_11.13 | all-reduce | flops 13152 | bytes 105216 | tf_op jit(solution)/shard_map/psum | solution.py:73
  (50 shorter events, 5.8 us)
Async XLA Ops:
  7.2 0.8 copy-start
  7.2 35.0 %copy-start.6 = (f32[48,128]{1,0:T(8,128)S(1)}, f32[48,128]{1,0:T(8,128)}, u32[]{:S(2)}) copy-start(f32[48,128]{1,0:T(8,128)} %param.8) | copy-start | bytes 73732
  7.2 182.1 %all-reduce.7.cloned.1.call-start = ((), (), s32[]{:S(2)}) async-start(), calls=%async_computation.6 | async-start | bytes 393216 | tf_op jit(solution)/shard_map/psum | solution.py:36
  45.0 575.7 %copy-start.7 = (s32[2]{0:T(128)S(1)}, s32[2]{0:T(128)}, u32[]{:S(2)}) copy-start(s32[2]{0:T(128)} %param.11) | copy-start | bytes 28
  45.7 210.2 %all-reduce.5.cloned.1.call-start = ((), (), s32[]{:S(2)}) async-start(), calls=%async_computation.3 | async-start | bytes 131072 | tf_op jit(solution)/shard_map/psum | solution.py:38
  189.3 99.8 %copy-start.4 = (f32[128,128]{0,1:T(8,128)S(1)}, f32[128,128]{0,1:T(8,128)}, u32[]{:S(2)}) copy-start(f32[128,128]{0,1:T(8,128)} %get-tuple-element.35) | copy-start | bytes 196612
  191.2 135.5 %reduce-scatter.3.cloned.1.call-start = ((), (), s32[]{:S(2)}) async-start(), calls=%async_computation.4 | async-start | bytes 3538944 | tf_op jit(solution)/shard_map/reduce_scatter | solution.py:41
  281.8 800.8 %copy-start.2 = (f32[128,192]{0,1:T(8,128)}, f32[128,192]{0,1:T(8,128)S(1)}, u32[]{:S(2)}) copy-start(f32[128,192]{0,1:T(8,128)S(1)} %fusion.15) | copy-start | bytes 294916
  288.9 256.7 %reduce-scatter.5.cloned.1.call-start = ((), (), s32[]{:S(2)}) async-start(), calls=%async_computation.5 | async-start | bytes 1081344 | tf_op jit(solution)/shard_map/reduce_scatter | solution.py:43
  312.4 750.7 %copy-start.5 = (f32[128,48]{0,1:T(8,128)}, f32[128,48]{0,1:T(8,128)S(1)}, u32[]{:S(2)}) copy-start(f32[128,48]{0,1:T(8,128)S(1)} %fusion.18) | copy-start | bytes 73732
  621.6 21.0 %copy-start.3 = (f32[2,4,16,128]{3,2,1,0:T(8,128)}, f32[2,4,16,128]{3,2,1,0:T(8,128)S(1)}, u32[]{:S(2)}) copy-start(f32[2,4,16,128]{3,2,1,0:T(8,128)S(1)} %fusion.12) | copy-start | bytes 196612
  642.6 8.7 copy-start.8
  642.6 413.7 %all-to-all-start = ((f32[32,2,4,128,128]{4,3,2,1,0:T(8,128)}), f32[32,2,4,128,128]{4,3,2,1,0:T(8,128)}, u32[]{:S(2)}, u32[]{:S(2)}) async-start(f32[32,2,4,128,128]{4,3,2,1,0:T(8,128)} %stack.22), calls=%async_computation.2 | async-start | bytes 33554432 | tf_op jit(solution)/shard_map/all_to_all | solution.py:50
  1082.7 58.2 %copy-start.1 = (f32[128,128]{1,0:T(8,128)S(1)}, f32[128,128]{1,0:T(8,128)}, u32[]{:S(2)}) copy-start(f32[128,128]{1,0:T(8,128)} %param.10) | copy-start | bytes 196612
Sparse Core Ops, SparseCore 0:
  45.9 143.3 all-reduce.6
  192.2 63.6 all-reduce.4
  289.0 37.6 reduce-scatter.2
  331.0 214.5 reduce-scatter.4
